TPU v7x, 32 devices: a whole 2x2x4 slice. The times are simulated.
32 devices in a mesh: row: 8 (over z, y), col: 4 (over x, core).
Axes of the slice: x: 2, y: 2, z: 4, core: 2. Of those that a mesh axis runs over, the one named last changes fastest.
Arguments:
- tokens: bfloat16 [2048, 4096], P('row', 'col'), may hold values from -6 to 6
- cotangent: bfloat16 [2048, 4096], P('row', 'col'), may hold values from -1.25 to 1.25
- w_up: float32 [4096, 12288], P('row', 'col'), may hold values from -0.1875 to 0.1875
- w_down: float32 [4096, 12288], P('row', 'col'), may hold values from -0.109375 to 0.109375
- mask_up: int32 [32, 96], P('row', 'col'), may hold values from 0 to 1, as said below
- mask_down: int32 [32, 96], P('row', 'col'), may hold values from 0 to 1, as said below
- moment_up: float32 [4096, 12288], P('row', 'col'), may hold values from -1.5 to 1.5
- second_up: float32 [4096, 12288], P('row', 'col'), may hold values from 0.01 to 0.2
- moment_down: float32 [4096, 12288], P('row', 'col'), may hold values from -1.5 to 1.5
- second_down: float32 [4096, 12288], P('row', 'col'), may hold values from 0.01 to 0.2
Outputs:
- token_grad: bfloat16 [2048, 4096], P('row', 'col')
- new_up: float32 [4096, 12288], P('row', 'col')
- new_moment_up: float32 [4096, 12288], P('row', 'col')
- new_second_up: float32 [4096, 12288], P('row', 'col')
- new_down: float32 [4096, 12288], P('row', 'col')
- new_moment_down: float32 [4096, 12288], P('row', 'col')
- new_second_down: float32 [4096, 12288], P('row', 'col')
Inputs may be any that keep to these rules, and one draw needn't show every extreme that they name: `mask_up`: 1 where the 128 x 128 block of the up projection is kept, else 0. Each tile of 4 x 24 blocks (the blocks of one device) holds at least 1 and at most 48 kept blocks, and some tile holds exactly 48. `mask_down`: 1 where the 128 x 128 block of the down projection is kept, else 0. Each tile of 4 x 24 blocks (the blocks of one device) holds at least 1 and at most 48 kept blocks, and some tile holds exactly 48.
All inputs are finite; a program needn't handle non-finite values.
Results may differ from a plain program's by a relative error of at most 0.018.
Values may be sent and summed in bfloat16 or wider, within the bound.
No kernel may reach another device: no remote copies, remote signals or barrier semaphores. Data moves between devices by JAX's collectives and lax.ppermute only.
A program may use at most 320 MiB of HBM per device.

v0:
```python
import jax
import jax.numpy as jnp
from jax import lax
from jax.sharding import PartitionSpec as P

inv_root_two = 0.7071067811865476
inv_root_two_pi = 0.3989422804014327
learn_rate = 0.001
bias_first = 1.0 - 0.9**10
bias_second = 1.0 - 0.95**10


def expand_mask(mask, block):
    blocks_r, blocks_c = mask.shape
    values = mask.astype(jnp.float32)[:, None, :, None]
    values = jnp.broadcast_to(values, (blocks_r, block, blocks_c, block))
    return values.reshape(blocks_r * block, blocks_c * block)


def gelu_parts(preact):
    normal_cdf = 0.5 * (1.0 + lax.erf(preact * inv_root_two))
    density = jnp.exp(-0.5 * preact * preact) * inv_root_two_pi
    return (preact * normal_cdf, normal_cdf + preact * density)


def adam_update(weight, moment, second, grad):
    moment_new = 0.9 * moment + 0.1 * grad
    second_new = 0.95 * second + 0.05 * grad * grad
    step_size = moment_new / bias_first / (jnp.sqrt(second_new / bias_second) + 1e-08)
    return (weight - learn_rate * step_size, moment_new, second_new)


def token_product(rows_full, other):
    return lax.dot_general(
        rows_full, other, (((0,), (0,)), ((), ())), preferred_element_type=jnp.float32
    )


def shards(
    tokens,
    cotangent,
    w_up,
    w_down,
    mask_up,
    mask_down,
    moment_up,
    second_up,
    moment_down,
    second_down,
):
    block = w_up.shape[0] // mask_up.shape[0]
    keep_up = expand_mask(mask_up, block)
    keep_down = expand_mask(mask_down, block)
    up_used = (w_up * keep_up).astype(jnp.bfloat16)
    down_used = (w_down * keep_down).astype(jnp.bfloat16)
    features, cot_rows = (
        lax.all_gather(tokens, "col", axis=1, tiled=True),
        lax.all_gather(cotangent, "col", axis=1, tiled=True),
    )
    up_whole = lax.all_gather(up_used, "row", axis=0, tiled=True)
    preact = jnp.dot(features, up_whole, preferred_element_type=jnp.float32)
    act_grad = jnp.dot(
        cot_rows,
        lax.all_gather(down_used, "row", axis=0, tiled=True),
        preferred_element_type=jnp.float32,
    )
    gelu_value, gelu_slope = gelu_parts(preact)
    activation = gelu_value.astype(jnp.bfloat16)
    pre_grad = (act_grad * gelu_slope).astype(jnp.bfloat16)
    partial_tokens = lax.dot_general(
        pre_grad, up_whole, (((1,), (1,)), ((), ())), preferred_element_type=jnp.float32
    )
    summed_down = lax.psum_scatter(
        token_product(cot_rows, activation).astype(jnp.bfloat16),
        "row",
        scatter_dimension=0,
        tiled=True,
    ).astype(jnp.float32)
    summed_up = lax.psum_scatter(
        token_product(features, pre_grad).astype(jnp.bfloat16),
        "row",
        scatter_dimension=0,
        tiled=True,
    ).astype(jnp.float32)
    token_grad = lax.psum_scatter(
        partial_tokens.astype(jnp.bfloat16), "col", scatter_dimension=1, tiled=True
    )
    grad_up = keep_up * summed_up
    grad_down = keep_down * summed_down
    new_up, new_moment_up, new_second_up = adam_update(w_up, moment_up, second_up, grad_up)
    new_down, new_moment_down, new_second_down = adam_update(
        w_down, moment_down, second_down, grad_down
    )
    return (
        token_grad,
        new_up,
        new_moment_up,
        new_second_up,
        new_down,
        new_moment_down,
        new_second_down,
    )


def solution(mesh):
    return jax.shard_map(
        shards,
        mesh=mesh,
        in_specs=(
            P("row", "col"),
            P("row", "col"),
            P("row", "col"),
            P("row", "col"),
            P("row", "col"),
            P("row", "col"),
            P("row", "col"),
            P("row", "col"),
            P("row", "col"),
            P("row", "col"),
        ),
        out_specs=(
            P("row", "col"),
            P("row", "col"),
            P("row", "col"),
            P("row", "col"),
            P("row", "col"),
            P("row", "col"),
            P("row", "col"),
        ),
        check_vma=False,
    )
```

profile of v0, /device:TPU:0, one launch (start us, length us, event | category | flops | bytes accessed | tf_op | source)
XLA Modules:
  0.0 1936.0 jit_solution(5846292603456907985)
XLA Ops:
  8.7 6.6 copy.20
  24.0 10.8 all-gather.11.cloned.1.call-done
  34.9 482.6 %all-gather.9.cloned.1.call-done = bf16[4096,3072]{0,1:T(8,128)(2,1)} async-done(((bf16[512,3072]{0,1:T(8,128)(2,1)}), bf16[4096,3072]{0,1:T(8,128)(2,1)}) %all-gather.9.cloned.1.call-update) | async-done | bytes 25165840 | tf_op jit(solution)/shard_map/all_gather | solution.py:60
  517.5 12.5 convolution_bitcast_fusion
  530.0 11.6 all-gather.7.cloned.1.call-done
  541.6 13.3 convert_bitcast_fusion
  562.2 7.0 copy.24
  569.3 6.6 copy.25
  575.8 383.7 %reduce-scatter.8.cloned.1.call-done = bf16[512,3072]{0,1:T(8,128)(2,1)} async-done(((bf16[4096,3072]{0,1:T(8,128)(2,1)}), bf16[512,3072]{0,1:T(8,128)(2,1)}) %reduce-scatter.8.cloned.1.call-update) | async-done | bytes 3145744 | tf_op jit(solution)/shard_map/reduce_scatter | solution.py:73
  964.6 15.1 multiply_subtract_fusion
  980.0 479.4 %all-gather.5.cloned.1.call-done = bf16[4096,3072]{0,1:T(8,128)(2,1)} async-done(((bf16[512,3072]{0,1:T(8,128)(2,1)}), bf16[4096,3072]{0,1:T(8,128)(2,1)}) %all-gather.5.cloned.1.call-update) | async-done | bytes 25165840 | tf_op jit(solution)/shard_map/all_gather | solution.py:64
  1459.4 13.6 fusion.5
  1473.1 13.3 convert_bitcast_fusion.1
  1486.7 14.3 convolution_convert_fusion
  1501.1 6.6 copy.21
  1507.7 6.6 copy.22
  1514.3 6.6 copy.30
  1520.8 6.6 copy.31
  1527.4 6.6 copy.32
  1534.0 356.8 %reduce-scatter.6.cloned.1.call-done = bf16[512,3072]{0,1:T(8,128)(2,1)} async-done(((bf16[4096,3072]{0,1:T(8,128)(2,1)}), bf16[512,3072]{0,1:T(8,128)(2,1)}) %reduce-scatter.6.cloned.1.call-update) | async-done | bytes 3145744 | tf_op jit(solution)/shard_map/reduce_scatter | solution.py:79
  1890.8 18.3 multiply_subtract_fusion.1
  1909.1 6.9 copy.27
  1916.0 6.6 copy.28
  1922.6 6.6 copy.29
  (33 shorter events, 23.2 us)
Async XLA Ops:
  7.2 27.7 %all-gather.11.cloned.1.call-start = ((), (), s32[]{:S(2)}) async-start(), calls=%async_computation.6 | async-start | bytes 2621440 | tf_op jit(solution)/shard_map/all_gather | solution.py:57
  7.9 509.6 %all-gather.9.cloned.1.call-start = ((), (), s32[]{:S(2)}) async-start(), calls=%async_computation.5 | async-start | bytes 28311552 | tf_op jit(solution)/shard_map/all_gather | solution.py:60
  15.3 5.1 copy-start
  16.2 3.2 copy-start.1
  23.2 518.4 %all-gather.7.cloned.1.call-start = ((), (), s32[]{:S(2)}) async-start(), calls=%async_computation.4 | async-start | bytes 2621440 | tf_op jit(solution)/shard_map/all_gather | solution.py:58
  24.0 935.5 %reduce-scatter.8.cloned.1.call-start = ((), (), s32[]{:S(2)}) async-start(), calls=%async_computation.9 | async-start | bytes 28311552 | tf_op jit(solution)/shard_map/reduce_scatter | solution.py:73
  530.0 24.9 %copy-start.3 = (f32[256,3072]{0,1:T(8,128)}, f32[256,3072]{0,1:T(8,128)S(1)}, u32[]{:S(2)}) copy-start(f32[256,3072]{0,1:T(8,128)S(1)} %convolution_bitcast_fusion) | copy-start | bytes 9437188
  554.9 0.7 copy-start.4
  554.9 904.5 %all-gather.5.cloned.1.call-start = ((), (), s32[]{:S(2)}) async-start(), calls=%async_computation.3 | async-start | bytes 28311552 | tf_op jit(solution)/shard_map/all_gather | solution.py:64
  959.5 5.1 copy-start.2
  979.8 911.0 %reduce-scatter.6.cloned.1.call-start = ((), (), s32[]{:S(2)}) async-start(), calls=%async_computation.8 | async-start | bytes 28311552 | tf_op jit(solution)/shard_map/reduce_scatter | solution.py:79
  1486.4 442.7 %reduce-scatter.4.cloned.1.call-start = ((), (), s32[]{:S(2)}) async-start(), calls=%async_computation.7 | async-start | bytes 2621440 | tf_op jit(solution)/shard_map/reduce_scatter | solution.py:85
Sparse Core Ops, SparseCore 0:
  9.6 25.2 all-gather.10
  37.0 480.4 all-gather.8
  519.0 22.5 all-gather.6
  555.1 404.4 reduce-scatter.7
  979.9 479.5 all-gather.4
  1486.5 404.2 reduce-scatter.5
  1893.9 30.5 reduce-scatter.3
where the time goes:
time: 1940 us
  waiting for transfers between devices  1730 us (89%)
  local copies, waits for them, and re-layouts  90.5 us (5%)
  matrix products  67.1 us (3%)
  other arithmetic  37 us (2%)
    all_gather x1, waiting for transfers between devices, shards(): up_whole = lax.all_gather(up_used, 'row', axis=0, tiled=True)  483 us
    all_gather x1, waiting for transfers between devices, shards(): lax.all_gather(down_used, 'row', axis=0, tiled=True)  479 us
    reduce_scatter x1, waiting for transfers between devices, shards(): lax.psum_scatter(token_product(cot_rows, activation).astype(jnp.bfloat16)...  384 us
    reduce_scatter x1, waiting for transfers between devices, shards(): lax.psum_scatter(token_product(features, pre_grad).astype(jnp.bfloat16),...  357 us
    unnamed x22, local copies, waits for them, and re-layouts  85.3 us
  transfers between devices with their start and end apart: 7, of which 6 were waited for; matrix products, arithmetic and copies ran while one was open for 7% of the time, Pallas kernels for 0%

commit v1 on v0

--- a/solution.py
+++ b/solution.py
@@ -57,7 +57,14 @@
         lax.all_gather(tokens, "col", axis=1, tiled=True),
         lax.all_gather(cotangent, "col", axis=1, tiled=True),
     )
-    up_whole = lax.all_gather(up_used, "row", axis=0, tiled=True)
+    ways, here = (lax.axis_size("row"), lax.axis_index("row"))
+    up_whole, reach = (up_used, 1)
+    while reach < ways:
+        theirs = lax.ppermute(up_whole, "row", [(d, d ^ reach) for d in range(ways)])
+        mine_first = jnp.concatenate([up_whole, theirs], axis=0)
+        theirs_first = jnp.concatenate([theirs, up_whole], axis=0)
+        up_whole = jnp.where(here & reach == 0, mine_first, theirs_first)
+        reach = 2 * reach
     preact = jnp.dot(features, up_whole, preferred_element_type=jnp.float32)
     act_grad = jnp.dot(
         cot_rows,

time: 1940 us -> 2210 us (1.14)
  waiting for transfers between devices: 1730 us -> 1950 us
  other arithmetic: 37 us -> 60.2 us
    ppermute x0 -> x3, waiting for transfers between devices: none -> 720 us  [shards(): lax.ppermute(up_whole, 'row', [(d, d ^ reach) for d in range(ways)])]
    all_gather x1 -> x0, waiting for transfers between devices: 483 us -> none  [shards(): up_whole = lax.all_gather(up_used, 'row', axis=0, tiled=True)]
    select_n x0 -> x2, other arithmetic: none -> 24.3 us  [shards(): up_whole = jnp.where(here & reach == 0, mine_first, theirs_first)]
    unnamed x22 -> x24, local copies, waits for them, and re-layouts: 85.3 us -> 85.3 us
  transfers between devices with their start and end apart: 7 -> 9, of which waited for: 6 -> 7; matrix products, arithmetic and copies ran while one was open for 7% -> 6% of each run, Pallas kernels for 0% -> 0%
where the time goes in v1:
time: 2210 us
  waiting for transfers between devices  1950 us (88%)
  local copies, waits for them, and re-layouts  90.4 us (4%)
  matrix products  89.1 us (4%)
  other arithmetic  60.2 us (3%)
    ppermute x3, waiting for transfers between devices, shards(): lax.ppermute(up_whole, 'row', [(d, d ^ reach) for d in range(ways)])  720 us
    all_gather x1, waiting for transfers between devices, shards(): lax.all_gather(down_used, 'row', axis=0, tiled=True)  479 us
    reduce_scatter x1, waiting for transfers between devices, shards(): lax.psum_scatter(token_product(cot_rows, activation).astype(jnp.bfloat16)...  384 us
    reduce_scatter x1, waiting for transfers between devices, shards(): lax.psum_scatter(token_product(features, pre_grad).astype(jnp.bfloat16),...  346 us
    unnamed x24, local copies, waits for them, and re-layouts  85.3 us
  transfers between devices with their start and end apart: 9, of which 7 were waited for; matrix products, arithmetic and copies ran while one was open for 6% of the time, Pallas kernels for 0%

profile of v1, /device:TPU:0, one launch (start us, length us, event | category | flops | bytes accessed | tf_op | source)
XLA Modules:
  0.0 2213.8 jit_solution(8141045959085610564)
XLA Ops:
  24.4 68.2 %collective-permute-done = bf16[512,3072]{0,1:T(8,128)(2,1)} collective-permute-done((bf16[512,3072]{0,1:T(8,128)(2,1)S(1)}, bf16[512,3072]{0,1:T(8,128)(2,1)}, u32[]{:S(2)}, u32[]{:S(2)}) %collective-permute-start) | collective-permute-done | bytes 3145760 | tf_op jit(solution)/shard_map/ppermute | solution.py:63
  92.6 8.1 maximum_select_fusion.2
  102.5 135.2 %collective-permute-done.1 = bf16[1024,3072]{0,1:T(8,128)(2,1)} collective-permute-done((bf16[1024,3072]{0,1:T(8,128)(2,1)}, bf16[1024,3072]{0,1:T(8,128)(2,1)}, u32[]{:S(2)}, u32[]{:S(2)}) %collective-permute-start.1) | collective-permute-done | bytes 6291488 | tf_op jit(solution)/shard_map/ppermute | solution.py:63
  237.7 16.2 maximum_select_fusion.1
  257.3 21.2 all-gather.8.cloned.1.call-done
  278.4 517.0 %collective-permute-done.2 = bf16[2048,3072]{0,1:T(8,128)(2,1)} collective-permute-done((bf16[2048,3072]{0,1:T(8,128)(2,1)}, bf16[2048,3072]{0,1:T(8,128)(2,1)}, u32[]{:S(2)}, u32[]{:S(2)}) %collective-permute-start.2) | collective-permute-done | bytes 12582944 | tf_op jit(solution)/shard_map/ppermute | solution.py:63
  795.4 21.8 fusion.5
  817.3 14.4 convert_bitcast_fusion
  839.0 7.0 copy.24
  846.1 6.6 copy.25
  852.6 384.2 %reduce-scatter.8.cloned.1.call-done = bf16[512,3072]{0,1:T(8,128)(2,1)} async-done(((bf16[4096,3072]{0,1:T(8,128)(2,1)}), bf16[512,3072]{0,1:T(8,128)(2,1)}) %reduce-scatter.8.cloned.1.call-update) | async-done | bytes 3145744 | tf_op jit(solution)/shard_map/reduce_scatter | solution.py:80
  1241.8 15.1 multiply_subtract_fusion
  1257.3 479.4 %all-gather.4.cloned.1.call-done = bf16[4096,3072]{0,1:T(8,128)(2,1)} async-done(((bf16[512,3072]{0,1:T(8,128)(2,1)}), bf16[4096,3072]{0,1:T(8,128)(2,1)}) %all-gather.4.cloned.1.call-update) | async-done | bytes 25165840 | tf_op jit(solution)/shard_map/all_gather | solution.py:71
  1736.7 13.4 convolution_bitcast_fusion
  1750.1 14.1 convert_bitcast_fusion.1
  1764.5 25.4 %convolution_convert_fusion = bf16[256,4096]{1,0:T(8,128)(2,1)} fusion(bf16[2048,3072]{0,1:T(8,128)(2,1)} %collective-permute-done.2, bf16[2048,3072]{0,1:T(8,128)(2,1)} %maximum_select_fusion.1, pred[]{:T(512)S(6)} %eq.9, f32[256,3072]{0,1:T(8,128)} %convolution_bitcast_fusion, f32[256,3072]{0,1:T(8,128)S(1)} %copy-done.4), kind=kOutput, calls=%fused_computation.19 | convolution fusion | flops 6564610048 | bytes 33554432 | tf_op jit(solution)/shard_map/dot_general | solution.py:77
  1790.0 6.6 copy.21
  1796.5 6.6 copy.22
  1803.2 6.6 copy.30
  1809.8 6.6 copy.31
  1816.3 6.6 copy.32
  1823.0 345.7 %reduce-scatter.6.cloned.1.call-done = bf16[512,3072]{0,1:T(8,128)(2,1)} async-done(((bf16[4096,3072]{0,1:T(8,128)(2,1)}), bf16[512,3072]{0,1:T(8,128)(2,1)}) %reduce-scatter.6.cloned.1.call-update) | async-done | bytes 3145744 | tf_op jit(solution)/shard_map/reduce_scatter | solution.py:86
  2168.7 18.3 multiply_subtract_fusion.1
  2187.0 6.9 copy.27
  (40 shorter events, 48.4 us)
Async XLA Ops:
  7.2 271.3 %all-gather.8.cloned.1.call-start = ((), (), s32[]{:S(2)}) async-start(), calls=%async_computation.5 | async-start | bytes 2621440 | tf_op jit(solution)/shard_map/all_gather | solution.py:57
  14.5 5.1 copy-start
  15.4 6.0 copy-start.1
  21.4 71.2 %collective-permute-start = (bf16[512,3072]{0,1:T(8,128)(2,1)S(1)}, bf16[512,3072]{0,1:T(8,128)(2,1)}, u32[]{:S(2)}, u32[]{:S(2)}) collective-permute-start(bf16[512,3072]{0,1:T(8,128)(2,1)S(1)} %fusion.2), channel_id=1, source_target_pairs={{0,4},{4,0},{8,12},{12,8},{16,20},{20,16},{24,28},{28,24},{1,5},{5... | collective-permute-start | bytes 9437192 | tf_op jit(solution)/shard_map/ppermute | solution.py:63
  100.7 137.0 %collective-permute-start.1 = (bf16[1024,3072]{0,1:T(8,128)(2,1)}, bf16[1024,3072]{0,1:T(8,128)(2,1)}, u32[]{:S(2)}, u32[]{:S(2)}) collective-permute-start(bf16[1024,3072]{0,1:T(8,128)(2,1)} %maximum_select_fusion.2), channel_id=1, source_target_pairs={{0,8},{4,12},{8,0},{12,4},{16,24},{20,28},{24,16},{28,20},{1,9},{5... | collective-permute-start | bytes 18874376 | tf_op jit(solution)/shard_map/ppermute | solution.py:63
  253.9 541.5 %collective-permute-start.2 = (bf16[2048,3072]{0,1:T(8,128)(2,1)}, bf16[2048,3072]{0,1:T(8,128)(2,1)}, u32[]{:S(2)}, u32[]{:S(2)}) collective-permute-start(bf16[2048,3072]{0,1:T(8,128)(2,1)} %maximum_select_fusion.1), channel_id=1, source_target_pairs={{0,16},{4,20},{8,24},{12,28},{16,0},{20,4},{24,8},{28,12},{1,17},{... | collective-permute-start | bytes 37748744 | tf_op jit(solution)/shard_map/ppermute | solution.py:63
  256.5 560.8 %all-gather.6.cloned.1.call-start = ((), (), s32[]{:S(2)}) async-start(), calls=%async_computation.4 | async-start | bytes 2621440 | tf_op jit(solution)/shard_map/all_gather | solution.py:58
  257.2 979.6 %reduce-scatter.8.cloned.1.call-start = ((), (), s32[]{:S(2)}) async-start(), calls=%async_computation.8 | async-start | bytes 28311552 | tf_op jit(solution)/shard_map/reduce_scatter | solution.py:80
  817.2 14.4 copy-start.3
  831.7 0.7 copy-start.5
  831.7 905.0 %all-gather.4.cloned.1.call-start = ((), (), s32[]{:S(2)}) async-start(), calls=%async_computation.3 | async-start | bytes 28311552 | tf_op jit(solution)/shard_map/all_gather | solution.py:71
  1236.8 5.1 copy-start.2
  1257.0 493.1 %copy-start.4 = (f32[256,3072]{0,1:T(8,128)S(1)}, f32[256,3072]{0,1:T(8,128)}, u32[]{:S(2)}) copy-start(f32[256,3072]{0,1:T(8,128)} %copy-done.3) | copy-start | bytes 9437188
  1257.0 911.7 %reduce-scatter.6.cloned.1.call-start = ((), (), s32[]{:S(2)}) async-start(), calls=%async_computation.7 | async-start | bytes 28311552 | tf_op jit(solution)/shard_map/reduce_scatter | solution.py:86
  1764.2 442.8 %reduce-scatter.4.cloned.1.call-start = ((), (), s32[]{:S(2)}) async-start(), calls=%async_computation.6 | async-start | bytes 2621440 | tf_op jit(solution)/shard_map/reduce_scatter | solution.py:92
Sparse Core Ops, SparseCore 0:
  256.6 21.7 all-gather.7
  280.0 22.5 all-gather.5
  831.8 404.9 reduce-scatter.7
  1257.1 479.5 all-gather.3
  1764.4 404.2 reduce-scatter.5
  2171.7 30.5 reduce-scatter.3
